TPU v7x, 256 devices: a whole 4x4x8 slice. The times are simulated.
256 devices in a mesh: dp: 32 (over z, y_hi, core), inner: 8 (over y_lo, x).
Axes of the slice: x: 4, y: 4 (y_hi: 2, y_lo: 2; y = y_hi * 2 + y_lo), z: 8, core: 2. Of those that a mesh axis runs over, the one named last changes fastest.
Arguments:
- tokens: bfloat16 [131072, 1664], P(('dp', 'inner')), may hold values from -16 to 16
- attn_gain: float32 [1664], replicated, may hold values from 0.1 to 1.9
- qkv_weight: bfloat16 [3, 1664, 832], P(None, 'dp', 'inner'), may hold values from -6 to 6
- out_weight: bfloat16 [832, 1664], P('inner', 'dp'), may hold values from -0.21875 to 0.21875
- merge_gain: float32 [6656], replicated, may hold values from 0.25 to 1.75
- merge_weight: bfloat16 [6656, 2048], P('dp', 'inner'), may hold values from -0.078125 to 0.078125
- segment_ids: int32 [131072], P('dp'), may hold values from -1 to 7, as said below
- owners: int32 [32768, 1], P('dp'), may hold values from 0 to 31; in each aligned block of 1024 rows (0 to 1023, 1024 to 2047, ...) at most 64 rows name the same one
Outputs:
- merged_out: bfloat16 [65536, 2048], P('dp', 'inner')
Inputs may be any that keep to these rules, and one draw needn't show every extreme that they name: `segment_ids`: within each device's aligned block of 512 tokens, ids never fall except to -1, which fills a tail of 4 or more tokens; every run of one id starts at a multiple of 4 and holds a multiple of 4 tokens. `owners`: in each aligned block of 1024 rows (the rows of one index of dp) no owner is named by more than 64 rows.
All inputs are finite; a program needn't handle non-finite values.
Results may differ from a plain program's by a relative error of at most 0.0062.
Values may be sent and summed in bfloat16 or wider, within the bound.
No kernel may reach another device: no remote copies, remote signals or barrier semaphores. Data moves between devices by JAX's collectives and lax.ppermute only.
A program may use at most 128 MiB of HBM per device.

v0:
```python
import jax
import jax.numpy as jnp
from jax import lax
from jax.sharding import PartitionSpec as P

HEAD_DIM = 104
EPS = 1e-06
NEG = -1e30


def layer_norm(values, gain):
    values = values.astype(jnp.float32)
    center = values - jnp.mean(values, axis=-1, keepdims=True)
    spread = jnp.mean(center * center, axis=-1, keepdims=True)
    return center * lax.rsqrt(spread + EPS) * gain


def attend_block(queries, keys, vectors, segment):
    scale = queries.shape[-1] ** (-0.5)
    scores = jnp.einsum("qhe,khe->hqk", queries, keys, preferred_element_type=jnp.float32) * scale
    visible = segment[:, None] == segment[None, :]
    scores = jnp.where(visible[None, :, :], scores, NEG)
    top = jnp.max(scores, axis=-1, keepdims=True)
    weights = jnp.exp(scores - top)
    probs = (weights / jnp.sum(weights, axis=-1, keepdims=True)).astype(jnp.bfloat16)
    context = jnp.einsum("hqk,khe->qhe", probs, vectors, preferred_element_type=jnp.float32)
    return context.astype(jnp.bfloat16)


def split_heads(projected):
    shaped = projected.reshape(3, projected.shape[1], projected.shape[2] // HEAD_DIM, HEAD_DIM)
    return (shaped[0], shaped[1], shaped[2])


def local(tokens, attn_gain, qkv_weight, out_weight, merge_gain, merge_weight, segment_ids, owners):
    tok_rows = tokens.shape[0]
    local_segment = lax.dynamic_slice_in_dim(
        segment_ids, lax.axis_index("inner") * tok_rows, tok_rows
    )
    normed = layer_norm(tokens, attn_gain).astype(jnp.bfloat16)
    qkv_part = lax.all_gather(qkv_weight, "inner", axis=2, tiled=True)
    projected = jnp.einsum(
        "td,cdh->cth",
        normed,
        lax.all_gather(qkv_part, "dp", axis=1, tiled=True),
        preferred_element_type=jnp.float32,
    )
    queries, keys, vectors = split_heads(projected.astype(jnp.bfloat16))
    context = attend_block(queries, keys, vectors, local_segment).reshape(tok_rows, -1)
    out_part = lax.all_gather(out_weight, "inner", axis=0, tiled=True)
    attn_out = jnp.dot(
        context,
        lax.all_gather(out_part, "dp", axis=1, tiled=True),
        preferred_element_type=jnp.float32,
    )
    hidden = tokens.astype(jnp.float32) + attn_out
    quad_rows = hidden.reshape(tok_rows // 4, -1)
    live = local_segment.reshape(-1, 4)[:, 0] >= 0
    merged = jnp.where(live[:, None], layer_norm(quad_rows, merge_gain), 0.0).astype(jnp.bfloat16)
    merge_full = lax.all_gather(merge_weight, "dp", axis=0, tiled=True)
    features = jnp.dot(
        lax.all_gather(merged, "inner", axis=0, tiled=True),
        merge_full,
        preferred_element_type=jnp.float32,
    ).astype(jnp.bfloat16)
    n_dp = lax.axis_size("dp")
    group_rows = features.shape[0]
    slots = 2 * group_rows // n_dp
    owner_col = owners[:, 0]
    chosen = (owner_col[:, None] == jnp.arange(n_dp, dtype=jnp.int32)[None, :]).astype(jnp.int32)
    earlier = jnp.cumsum(chosen, axis=0) - chosen
    rank = jnp.sum(earlier * chosen, axis=1)
    target = owner_col * slots + rank
    source_row = (
        jnp.full((n_dp * slots,), group_rows, jnp.int32)
        .at[target]
        .set(jnp.arange(group_rows, dtype=jnp.int32))
    )
    padded = jnp.concatenate([features, jnp.zeros((1, features.shape[1]), jnp.bfloat16)], axis=0)
    outgoing = padded[source_row]
    return lax.all_to_all(outgoing, "dp", split_axis=0, concat_axis=0, tiled=True)


def solution(mesh):
    placed = (
        P(("dp", "inner"), None),
        P(),
        P(None, "dp", "inner"),
        P("inner", "dp"),
        P(),
        P("dp", "inner"),
        P("dp"),
        P("dp", None),
    )
    return jax.shard_map(
        local, mesh=mesh, in_specs=placed, out_specs=P("dp", "inner"), check_vma=False
    )
```

profile of v0, /device:TPU:1, one launch (start us, length us, event | category | flops | bytes accessed | tf_op | source)
XLA Modules:
  0.0 524.1 jit_solution(5814935744648838367)
XLA Ops:
  6.5 23.5 %all-gather = bf16[8,104,52]{1,2,0:T(8,128)(2,1)S(1)} all-gather(bf16[1,104,52]{1,2,0:T(8,128)(2,1)} %bitcast.61), channel_id=1, replica_groups=mesh['dp'=32,'inner'=8] {'inner'}, dimensions={0}, use_global_device_ids=true | all-gather | bytes 97344 | tf_op jit(solution)/shard_map/all_gather | solution.py:50
  30.0 0.8 reshape.115
  30.8 0.0 all-gather.13.cloned.1.call-update
  30.8 0.0 all-gather.7.cloned.1.call-start
  30.9 0.9 copy.18
  31.8 24.0 %all_gather.18 = bf16[3,52,832]{1,0,2:T(4,128)(2,1)S(1)} all-gather(bf16[3,52,104]{1,0,2:T(4,128)(2,1)S(1)} %copy.18), channel_id=1, replica_groups=mesh['dp'=32,'inner'=8] {'inner'}, dimensions={2}, use_global_device_ids=true | all-gather | bytes 292032 | tf_op jit(solution)/shard_map/all_gather | solution.py:41
  55.8 1.7 copy.19
  57.5 0.0 all-gather.7.cloned.1.call-update
  57.6 0.0 all-gather.11.cloned.1.call-start
  57.6 0.7 all-gather.11.cloned.1.call-update
  58.3 0.0 all-gather.9.cloned.1.call-start
  58.3 0.3 convert_reduce_fusion
  58.7 0.6 fusion.10
  59.3 0.8 dynamic_slice.3
  60.0 0.1 reshape.93
  60.1 0.1 fusion.27
  60.3 0.9 broadcast_compare_fusion
  61.2 62.0 %all-gather.13.cloned.1.call-done = bf16[32,52,832]{2,1,0:T(8,128)(2,1)} async-done(((bf16[1,52,832]{2,1,0:T(8,128)(2,1)}), bf16[32,52,832]{2,1,0:T(8,128)(2,1)}) %all-gather.13.cloned.1.call-update) | async-done | bytes 2768912 | tf_op jit(solution)/shard_map/all_gather | solution.py:53
  123.2 5.6 %reshape.117 = bf16[1664,832]{1,0:T(8,128)(2,1)} reshape(bf16[32,52,832]{2,1,0:T(8,128)(2,1)} %all-gather.13.cloned.1.call-done) | data formatting | bytes 5537792
  128.8 108.2 %all-gather.7.cloned.1.call-done = bf16[3,1664,832]{2,0,1:T(4,128)(2,1)} async-done(((bf16[3,52,832]{2,0,1:T(4,128)(2,1)}), bf16[3,1664,832]{2,0,1:T(4,128)(2,1)}) %all-gather.7.cloned.1.call-update) | async-done | bytes 8306704 | tf_op jit(solution)/shard_map/all_gather | solution.py:45
  237.0 12.2 %convert_bitcast_fusion = bf16[3,512,832]{1,2,0:T(8,128)(2,1)S(1)} fusion(bf16[3,1664,832]{2,0,1:T(4,128)(2,1)} %all-gather.7.cloned.1.call-done, bf16[512,1664]{1,0:T(8,128)(2,1)S(1)} %copy-done, f32[1664]{0:T(1024)S(1)} %copy-done.4, f32[512]{0:T(512)S(1)} %add_rsqrt_fusion, f32[512]{0:T(512)S(1)} %broadcast_multiply_fusion), kind=kOutput, calls=%fused_computation.23 | convolution fusion | flops 4258562048 | bytes 12577280 | tf_op jit(solution)/shard_map/td,cdh->cth/dot_general | solution.py:42
  249.2 1.1 fusion.33
  250.3 7.8 %fusion.34 = (f32[8,512]{1,0:T(8,128)S(1)}, f32[8,512,512]{1,2,0:T(8,128)}) fusion(pred[512,512]{0,1:T(8,128)(4,1)} %broadcast_compare_fusion, bf16[512,8,104]{0,2,1:T(8,128)(2,1)} %bitcast.54, bf16[512,8,104]{0,2,1:T(8,128)(2,1)S(1)} %bitcast.53), kind=kOutput, calls=%fused_computation.54 | convolution fusion | flops 444596736 | bytes 10371072 | tf_op jit(solution)/shard_map/sub | solution.py:24
  258.1 4.3 fusion.20
  262.4 3.9 fusion.35
  266.3 0.1 reduce_sum.74
  266.4 0.1 reduce_sum.75
  266.5 0.1 sub.42
  266.6 0.1 sub.43
  266.7 2.9 reshape.95
  269.7 0.0 copy-start.3
  269.7 2.4 multiply_reduce_fusion
  272.1 0.1 reduce_sum.77
  272.2 0.1 reduce_sum.78
  272.4 1.8 select_convert_fusion
  274.2 0.0 all-gather.9.cloned.1.call-update
  274.2 9.2 %reduce-window.6 = s32[32,8,128]{2,1,0:T(8,128)S(1)} reduce-window(s32[32,8,128]{2,1,0:T(8,128)S(1)} %fusion.26, s32[]{:T(128)} %constant.18.clone.1), window={size=1x1x128 pad=0_0x0_0x127_0}, to_apply=%region_8.9 | reduce-window | flops 4161536 | bytes 262148 | tf_op jit(solution)/shard_map/reduce-window
  283.4 0.1 slice.33
  283.5 0.1 copy.23
  283.7 0.1 copy.24
  283.8 0.1 broadcast_add_fusion
  284.0 4.3 scatter_custom_fusion
  288.3 32.0 %all-gather.11.cloned.1.call-done = bf16[6656,256]{1,0:T(8,128)(2,1)} async-done(((bf16[208,256]{1,0:T(8,128)(2,1)}), bf16[6656,256]{1,0:T(8,128)(2,1)}) %all-gather.11.cloned.1.call-update) | async-done | bytes 3407888 | tf_op jit(solution)/shard_map/all_gather | solution.py:60
  320.3 141.2 %all-gather.9.cloned.1.call-done = bf16[1024,6656]{1,0:T(8,128)(2,1)} async-done(((bf16[128,6656]{1,0:T(8,128)(2,1)}), bf16[1024,6656]{1,0:T(8,128)(2,1)}) %all-gather.9.cloned.1.call-update) | async-done | bytes 13631504 | tf_op jit(solution)/shard_map/all_gather | solution.py:62
  461.5 9.5 %convolution_convert_fusion = bf16[1024,256]{1,0:T(8,128)(2,1)S(1)} fusion(bf16[1024,6656]{1,0:T(8,128)(2,1)} %all-gather.9.cloned.1.call-done, bf16[6656,256]{1,0:T(8,128)(2,1)} %all-gather.11.cloned.1.call-done), kind=kOutput, calls=%fused_computation.29 | convolution fusion | flops 3489923072 | bytes 17563648 | tf_op jit(solution)/shard_map/dot_general | solution.py:61
  471.1 7.5 %gather_fusion = bf16[2048,256]{1,0:T(8,128)(2,1)S(1)} fusion(bf16[1025,256]{1,0:T(8,128)(2,1)S(1)} %concatenate.3, s32[2048]{0:T(1024)S(1)} %fusion.28), kind=kCustom, calls=%fused_computation | custom fusion | bytes 2105344 | tf_op jit(solution)/shard_map/gather | solution.py:80
  478.6 38.0 %all_to_all.12 = bf16[32,64,256]{2,1,0:T(8,128)(2,1)S(1)} all-to-all(bf16[32,64,256]{2,1,0:T(8,128)(2,1)S(1)} %bitcast.51), channel_id=1, replica_groups=mesh['dp'=32,'inner'=8] {'dp'}, dimensions={0} | all-to-all | bytes 2097152 | tf_op jit(solution)/shard_map/all_to_all | solution.py:81
  516.6 1.0 copy.33
  (23 shorter events, 0.2 us)
Async XLA Ops:
  6.5 51.8 %copy-start = (bf16[512,1664]{1,0:T(8,128)(2,1)S(1)}, bf16[512,1664]{1,0:T(8,128)(2,1)}, u32[]{:S(2)}) copy-start(bf16[512,1664]{1,0:T(8,128)(2,1)} %param.8) | copy-start | bytes 5111812
  6.5 116.6 %all-gather.13.cloned.1.call-start = ((), (), s32[]{:S(2)}) async-start(), calls=%async_computation.4 | async-start | bytes 3311616 | tf_op jit(solution)/shard_map/all_gather | solution.py:53
  30.8 206.1 %all-gather.7.cloned.1.call-start = ((), (), s32[]{:S(2)}) async-start(), calls=%async_computation.1 | async-start | bytes 12300288 | tf_op jit(solution)/shard_map/all_gather | solution.py:45
  57.6 262.8 %all-gather.11.cloned.1.call-start = ((), (), s32[]{:S(2)}) async-start(), calls=%async_computation.3 | async-start | bytes 3514368 | tf_op jit(solution)/shard_map/all_gather | solution.py:60
  58.3 403.2 %all-gather.9.cloned.1.call-start = ((), (), s32[]{:S(2)}) async-start(), calls=%async_computation.2 | async-start | bytes 15335424 | tf_op jit(solution)/shard_map/all_gather | solution.py:62
  59.2 177.7 %copy-start.4 = (f32[1664]{0:T(1024)S(1)}, f32[1664]{0:T(1024)}, u32[]{:S(2)}) copy-start(f32[1664]{0:T(1024)} %param.9) | copy-start | bytes 19972
  258.1 4.3 copy-start.1
  269.7 2.7 copy-start.3
  272.4 1.8 copy-start.2
Sparse Core Ops, SparseCore 0:
  31.0 92.1 all-gather.12
  125.9 111.0 all-gather.6
  239.8 80.5 all-gather.10
  322.0 139.5 all-gather.8
where the time goes:
time: 525 us; the launch traced here: 524 us
  waiting for transfers between devices  344 us (66%)
  blocking collectives  85.5 us (16%)
  matrix products  37.7 us (7%)
  local copies, waits for them, and re-layouts  27.6 us (5%)
  other arithmetic  15.8 us (3%)
  between operations  13.4 us (3%)
    all_gather x1, waiting for transfers between devices, local(): lax.all_gather(merged, 'inner', axis=0, tiled=True)  141 us
    all_gather x1, waiting for transfers between devices, local(): lax.all_gather(qkv_part, 'dp', axis=1, tiled=True)  108 us
    all_gather x1, waiting for transfers between devices, local(): lax.all_gather(out_part, 'dp', axis=1, tiled=True)  62 us
    all_to_all x1, blocking collectives, local(): lax.all_to_all(outgoing, 'dp', split_axis=0, concat_axis=0, tiled=True)  38 us
    all_gather x1, waiting for transfers between devices, local(): merge_full = lax.all_gather(merge_weight, 'dp', axis=0, tiled=True)  32 us
    all_gather x1, blocking collectives, local(): qkv_part = lax.all_gather(qkv_weight, 'inner', axis=2, tiled=True)  24 us
    all_gather x1, blocking collectives, local(): out_part = lax.all_gather(out_weight, 'inner', axis=0, tiled=True)  23.5 us
    dot_general x1, matrix products, local(): jnp.einsum('td,cdh->cth', normed, lax.all_gather(qkv_part, 'dp', axis=1,...  12.2 us
  transfers between devices with their start and end apart: 4, of which 4 were waited for; matrix products, arithmetic and copies ran while one was open for 12% of the time, Pallas kernels for 0%

commit v1 on v0

--- a/solution.py
+++ b/solution.py
@@ -59,7 +59,9 @@
     merged = jnp.where(live[:, None], layer_norm(quad_rows, merge_gain), 0.0).astype(jnp.bfloat16)
     merge_full = lax.all_gather(merge_weight, "dp", axis=0, tiled=True)
     features = jnp.dot(
-        lax.all_gather(merged, "inner", axis=0, tiled=True),
+        jnp.concatenate(
+            lax.all_to_all(jnp.stack([merged] * lax.axis_size("inner")), "inner", 0, 0), axis=0
+        ),
         merge_full,
         preferred_element_type=jnp.float32,
     ).astype(jnp.bfloat16)

time: 525 us -> 550 us (1.048)
  the two profiles are of different devices: /device:TPU:1 before, /device:TPU:30 now
where the time goes in v1:
time: 550 us; the launch traced here: 549 us
  waiting for transfers between devices  347 us (63%)
  blocking collectives  94.6 us (17%)
  matrix products  37.5 us (7%)
  local copies, waits for them, and re-layouts  35.3 us (6%)
  other arithmetic  15.6 us (3%)
  between operations  13.3 us (2%)
  starting transfers between devices  5.88 us (1%)
    all_gather x1, waiting for transfers between devices, local(): merge_full = lax.all_gather(merge_weight, 'dp', axis=0, tiled=True)  185 us
    all_gather x1, waiting for transfers between devices, local(): lax.all_gather(qkv_part, 'dp', axis=1, tiled=True)  108 us
    all_gather x1, waiting for transfers between devices, local(): lax.all_gather(out_part, 'dp', axis=1, tiled=True)  48.7 us
    all_to_all x1, blocking collectives, local(): lax.all_to_all(outgoing, 'dp', split_axis=0, concat_axis=0, tiled=True)  36.2 us
    all_gather x1, blocking collectives, local(): qkv_part = lax.all_gather(qkv_weight, 'inner', axis=2, tiled=True)  29.9 us
    all_gather x1, blocking collectives, local(): out_part = lax.all_gather(out_weight, 'inner', axis=0, tiled=True)  28.6 us
    dot_general x1, matrix products, local(): jnp.einsum('td,cdh->cth', normed, lax.all_gather(qkv_part, 'dp', axis=1,...  12.2 us
  transfers between devices with their start and end apart: 4, of which 4 were waited for; matrix products, arithmetic and copies ran while one was open for 5% of the time, Pallas kernels for 0%

profile of v1, /device:TPU:30, one launch (start us, length us, event | category | flops | bytes accessed | tf_op | source)
XLA Modules:
  0.0 549.3 jit_solution(15806895018662957013)
XLA Ops:
  6.5 28.6 %all-gather = bf16[8,104,52]{1,2,0:T(8,128)(2,1)S(1)} all-gather(bf16[1,104,52]{1,2,0:T(8,128)(2,1)} %bitcast.62), channel_id=1, replica_groups=mesh['dp'=32,'inner'=8] {'inner'}, dimensions={0}, use_global_device_ids=true | all-gather | bytes 97344 | tf_op jit(solution)/shard_map/all_gather | solution.py:50
  35.1 0.8 reshape.149
  35.9 0.0 all-gather.10.cloned.1.call-update
  35.9 0.0 all-gather.6.cloned.1.call-start
  36.0 0.9 copy.18
  36.9 29.9 %all_gather.15 = bf16[3,52,832]{1,0,2:T(4,128)(2,1)S(1)} all-gather(bf16[3,52,104]{1,0,2:T(4,128)(2,1)S(1)} %copy.18), channel_id=1, replica_groups=mesh['dp'=32,'inner'=8] {'inner'}, dimensions={2}, use_global_device_ids=true | all-gather | bytes 292032 | tf_op jit(solution)/shard_map/all_gather | solution.py:41
  66.8 1.7 copy.19
  68.5 0.0 all-gather.6.cloned.1.call-update
  68.5 0.8 dynamic_slice.3
  69.3 0.1 reshape.126
  69.4 0.1 fusion.27
  69.5 0.3 convert_reduce_fusion
  69.8 0.6 fusion.10
  70.4 0.9 broadcast_compare_fusion
  71.4 48.7 %all-gather.10.cloned.1.call-done = bf16[32,52,832]{2,1,0:T(8,128)(2,1)} async-done(((bf16[1,52,832]{2,1,0:T(8,128)(2,1)}), bf16[32,52,832]{2,1,0:T(8,128)(2,1)}) %all-gather.10.cloned.1.call-update) | async-done | bytes 2768912 | tf_op jit(solution)/shard_map/all_gather | solution.py:53
  120.0 5.7 %reshape.151 = bf16[1664,832]{1,0:T(8,128)(2,1)} reshape(bf16[32,52,832]{2,1,0:T(8,128)(2,1)} %all-gather.10.cloned.1.call-done) | data formatting | bytes 5537792
  125.7 108.1 %all-gather.6.cloned.1.call-done = bf16[3,1664,832]{2,0,1:T(4,128)(2,1)} async-done(((bf16[3,52,832]{2,0,1:T(4,128)(2,1)}), bf16[3,1664,832]{2,0,1:T(4,128)(2,1)}) %all-gather.6.cloned.1.call-update) | async-done | bytes 8306704 | tf_op jit(solution)/shard_map/all_gather | solution.py:45
  233.8 12.2 %convert_bitcast_fusion = bf16[3,512,832]{1,2,0:T(8,128)(2,1)S(1)} fusion(bf16[3,1664,832]{2,0,1:T(4,128)(2,1)} %all-gather.6.cloned.1.call-done, bf16[512,1664]{1,0:T(8,128)(2,1)S(1)} %copy-done, f32[1664]{0:T(1024)S(1)} %copy-done.4, f32[512]{0:T(512)S(1)} %add_rsqrt_fusion, f32[512]{0:T(512)S(1)} %broadcast_multiply_fusion), kind=kOutput, calls=%fused_computation.23 | convolution fusion | flops 4258562048 | bytes 12577280 | tf_op jit(solution)/shard_map/td,cdh->cth/dot_general | solution.py:42
  246.0 1.1 fusion.33
  247.1 7.6 %fusion.34 = (f32[8,512]{1,0:T(8,128)S(1)}, f32[8,512,512]{1,2,0:T(8,128)}) fusion(pred[512,512]{0,1:T(8,128)(4,1)} %broadcast_compare_fusion, bf16[512,8,104]{0,2,1:T(8,128)(2,1)} %bitcast.55, bf16[512,8,104]{0,2,1:T(8,128)(2,1)S(1)} %bitcast.54), kind=kOutput, calls=%fused_computation.54 | convolution fusion | flops 444596736 | bytes 10371072 | tf_op jit(solution)/shard_map/sub | solution.py:24
  254.8 4.3 fusion.20
  259.1 0.0 copy-done.1
  259.1 3.8 fusion.35
  262.9 0.1 reduce_sum.74
  263.0 0.1 reduce_sum.75
  263.2 0.1 sub.44
  263.2 0.1 sub.45
  263.4 3.1 reshape.128
  266.5 0.0 copy-start.3
  266.5 2.4 multiply_reduce_fusion
  268.9 0.1 reduce_sum.77
  269.0 0.1 reduce_sum.78
  269.2 1.8 select_convert_fusion
  271.0 7.5 %stack.2 = bf16[8,128,6656]{2,1,0:T(8,128)(2,1)} broadcast(bf16[128,6656]{1,0:T(8,128)(2,1)} %select_convert_fusion), dimensions={1,2} | broadcast | bytes 15335424 | tf_op jit(solution)/shard_map/stack | solution.py:63
  278.4 5.8 %all-to-all-start = ((bf16[8,128,6656]{2,1,0:T(8,128)(2,1)}), bf16[8,128,6656]{2,1,0:T(8,128)(2,1)}, u32[]{:S(2)}, u32[]{:S(2)}) async-start(bf16[8,128,6656]{2,1,0:T(8,128)(2,1)} %stack.2), calls=%async_computation | async-start | bytes 27262976 | tf_op jit(solution)/shard_map/all_to_all | solution.py:63
  284.3 0.7 all-gather.8.cloned.1.call-update
  285.0 9.0 %reduce-window.6 = s32[32,8,128]{2,1,0:T(8,128)S(1)} reduce-window(s32[32,8,128]{2,1,0:T(8,128)S(1)} %fusion.26, s32[]{:T(128)} %constant.18.clone.1), window={size=1x1x128 pad=0_0x0_0x127_0}, to_apply=%region_8.9 | reduce-window | flops 4161536 | bytes 262148 | tf_op jit(solution)/shard_map/reduce-window
  294.1 0.1 slice.33
  294.1 0.1 copy.23
  294.3 0.1 copy.24
  294.4 0.1 broadcast_add_fusion
  294.6 4.3 scatter_custom_fusion
  298.9 185.3 %all-gather.8.cloned.1.call-done = bf16[6656,256]{1,0:T(8,128)(2,1)} async-done(((bf16[208,256]{1,0:T(8,128)(2,1)}), bf16[6656,256]{1,0:T(8,128)(2,1)}) %all-gather.8.cloned.1.call-update) | async-done | bytes 3407888 | tf_op jit(solution)/shard_map/all_gather | solution.py:60
  484.2 4.2 all-to-all-done
  488.5 9.5 %convolution_convert_fusion = bf16[1024,256]{1,0:T(8,128)(2,1)S(1)} fusion(bf16[1024,6656]{1,0:T(8,128)(2,1)} %bitcast.10, bf16[6656,256]{1,0:T(8,128)(2,1)} %all-gather.8.cloned.1.call-done), kind=kOutput, calls=%fused_computation.29 | convolution fusion | flops 3489923072 | bytes 17563648 | tf_op jit(solution)/shard_map/dot_general | solution.py:61
  498.1 7.5 %gather_fusion = bf16[2048,256]{1,0:T(8,128)(2,1)S(1)} fusion(bf16[1025,256]{1,0:T(8,128)(2,1)S(1)} %concatenate.3, s32[2048]{0:T(1024)S(1)} %fusion.28), kind=kCustom, calls=%fused_computation | custom fusion | bytes 2105344 | tf_op jit(solution)/shard_map/gather | solution.py:82
  505.6 36.2 %all_to_all.17 = bf16[32,64,256]{2,1,0:T(8,128)(2,1)S(1)} all-to-all(bf16[32,64,256]{2,1,0:T(8,128)(2,1)S(1)} %bitcast.52), channel_id=1, replica_groups=mesh['dp'=32,'inner'=8] {'dp'}, dimensions={0} | all-to-all | bytes 2097152 | tf_op jit(solution)/shard_map/all_to_all | solution.py:83
  541.8 1.0 copy.33
  (23 shorter events, 0.2 us)
Async XLA Ops:
  6.5 63.0 %copy-start = (bf16[512,1664]{1,0:T(8,128)(2,1)S(1)}, bf16[512,1664]{1,0:T(8,128)(2,1)}, u32[]{:S(2)}) copy-start(bf16[512,1664]{1,0:T(8,128)(2,1)} %param.8) | copy-start | bytes 5111812
  6.5 113.5 %all-gather.10.cloned.1.call-start = ((), (), s32[]{:S(2)}) async-start(), calls=%async_computation.4 | async-start | bytes 3311616 | tf_op jit(solution)/shard_map/all_gather | solution.py:53
  35.9 197.9 %all-gather.6.cloned.1.call-start = ((), (), s32[]{:S(2)}) async-start(), calls=%async_computation.2 | async-start | bytes 12300288 | tf_op jit(solution)/shard_map/all_gather | solution.py:45
  70.4 163.4 %copy-start.4 = (f32[1664]{0:T(1024)S(1)}, f32[1664]{0:T(1024)}, u32[]{:S(2)}) copy-start(f32[1664]{0:T(1024)} %param.9) | copy-start | bytes 19972
  254.8 4.3 copy-start.1
  266.5 2.7 copy-start.3
  278.4 6.6 %copy-start.2 = (s32[1024,1]{0,1:T(1,128)S(1)}, s32[1024,1]{0,1:T(1,128)}, u32[]{:S(2)}) copy-start(s32[1024,1]{0,1:T(1,128)} %param.15) | copy-start | bytes 12292
  278.4 210.0 %all-to-all-start = ((bf16[8,128,6656]{2,1,0:T(8,128)(2,1)}), bf16[8,128,6656]{2,1,0:T(8,128)(2,1)}, u32[]{:S(2)}, u32[]{:S(2)}) async-start(bf16[8,128,6656]{2,1,0:T(8,128)(2,1)} %stack.2), calls=%async_computation | async-start | bytes 27262976 | tf_op jit(solution)/shard_map/all_to_all | solution.py:63
  284.3 200.0 %all-gather.8.cloned.1.call-start = ((), (), s32[]{:S(2)}) async-start(), calls=%async_computation.3 | async-start | bytes 3514368 | tf_op jit(solution)/shard_map/all_gather | solution.py:60
Sparse Core Ops, SparseCore 0:
  36.0 83.9 all-gather.9
  122.8 111.0 all-gather.5
  287.8 196.3 all-gather.7
